TPU v7x, 512 devices: a whole 4x4x16 slice. The times are simulated.
512 devices in a mesh: blk: 64 (over y_lo, z, core), exp: 8 (over y_hi, x).
Axes of the slice: x: 4, y: 4 (y_hi: 2, y_lo: 2; y = y_hi * 2 + y_lo), z: 16, core: 2. Of those that a mesh axis runs over, the one named last changes fastest.
Arguments:
- hidden_in: bfloat16 [32, 4, 2048], P('exp'), may hold values from -3 to 3
- q_lat: bfloat16 [32, 4, 16, 512], P('exp'), may hold values from -28 to 28
- q_rope: bfloat16 [32, 4, 16, 64], P('exp'), may hold values from -4 to 4
- new_lat: bfloat16 [32, 4, 512], P('exp'), may hold values from -4 to 4
- new_rope: bfloat16 [32, 4, 64], P('exp'), may hold values from -4 to 4
- cache_lat: bfloat16 [32, 16384, 512], P('exp', 'blk'), may hold values from -4 to 4
- cache_rope: bfloat16 [32, 16384, 64], P('exp', 'blk'), may hold values from -4 to 4
- lengths: int32 [32], P('exp'), may hold values from 2 to 16384, as said below
- w_uv: bfloat16 [512, 2048], P(None, 'blk'), may hold values from -3 to 3
- w_out: bfloat16 [2048, 2048], P('blk'), may hold values from -0.125 to 0.125
- norm_gain: float32 [2048], replicated, may hold values from 0.1 to 1.9
- w_router: bfloat16 [2048, 64], replicated, may hold values from -0.125 to 0.125
- routes: int32 [32, 4, 6], P('exp'), may hold values from 0 to 63, all different within a row; in each aligned block of 16 rows (0 to 15, 16 to 31, ..., all dimensions but the last counted through in order) at most 3 rows name the same one
- w_gate: bfloat16 [64, 2048, 1408], P('blk', None, 'exp'), may hold values from -0.125 to 0.125
- w_up: bfloat16 [64, 2048, 1408], P('blk', None, 'exp'), may hold values from -0.125 to 0.125
- w_down: bfloat16 [64, 1408, 2048], P('blk', 'exp'), may hold values from -0.15625 to 0.15625
Outputs:
- hidden_out: bfloat16 [32, 4, 2048], P('exp')
Inputs may be any that keep to these rules, and one draw needn't show every extreme that they name: `lengths`: in each aligned group of 4 requests exactly 1 have length 16384; the others have 2 to 512. `routes`: each row names 6 different experts; in the 16 rows of one index of exp no expert is named more than 3 times.
All inputs are finite; a program needn't handle non-finite values.
Results may differ from a plain program's by a relative error of at most 0.0062.
Values may be sent and summed in bfloat16 or wider, within the bound.
No kernel may reach another device: no remote copies, remote signals or barrier semaphores. Data moves between devices by JAX's collectives and lax.ppermute only.
A program may use at most 128 MiB of HBM per device.

v0:
```python
import jax
import jax.numpy as jnp
from jax import lax
from jax.sharding import PartitionSpec as P

V = 128
QK = 192
CAP = 3
NEG_FILL = -1e30
ROUTE_SCALE = 2.446
NORM_EPS = 1e-06


def merged_2(x, axis, combine):
    everything = jax.tree.map(lambda part: lax.all_gather(part, axis), x)
    leading = jax.tree.map(lambda part: part[0], everything)

    def step(k, so_far):
        return combine(so_far, jax.tree.map(lambda part: part[k], everything))

    return lax.fori_loop(1, lax.axis_size(axis), step, leading)


def block_partial(query, query_rope, keys_lat, keys_rope, valid):
    scale = QK ** (-0.5)
    scores = (
        jnp.einsum("rmc,rkc->rmk", query, keys_lat, preferred_element_type=jnp.float32)
        + jnp.einsum("rmc,rkc->rmk", query_rope, keys_rope, preferred_element_type=jnp.float32)
    ) * scale
    masked = jnp.where(valid, scores, NEG_FILL)
    peak_val = jnp.max(masked, axis=2)
    weights = jnp.where(valid, jnp.exp(masked - peak_val[:, :, None]), 0.0)
    weight_sum = jnp.sum(weights, axis=2)
    summed = jnp.einsum(
        "rmk,rkc->rmc", weights.astype(jnp.bfloat16), keys_lat, preferred_element_type=jnp.float32
    )
    return (peak_val, weight_sum, summed)


def merge_pair(left_part, right_part):
    peak_left, total_left, sum_left = left_part
    peak_right, total_right, sum_right = right_part
    peak_val = jnp.maximum(peak_left, peak_right)
    factor_left = jnp.exp(peak_left - peak_val)
    factor_right = jnp.exp(peak_right - peak_val)
    weight_sum = factor_left * total_left + factor_right * total_right
    summed = factor_left[..., None] * sum_left + factor_right[..., None] * sum_right
    return (peak_val, weight_sum, summed)


def local(
    hidden_in,
    q_lat,
    q_rope,
    new_lat,
    new_rope,
    cache_lat,
    cache_rope,
    lengths,
    w_uv,
    w_out,
    norm_gain,
    w_router,
    routes,
    w_gate,
    w_up,
    w_down,
):
    requests, new_steps, head_count, latent_dim = q_lat.shape
    query_rows = new_steps * head_count
    query = q_lat.reshape(requests, query_rows, latent_dim)
    query_rope = q_rope.reshape(requests, query_rows, q_rope.shape[3])
    cache_span = cache_lat.shape[1]
    position = lax.axis_index("blk") * cache_span + lax.iota(jnp.int32, cache_span)
    cache_valid = jnp.broadcast_to(
        position[None, None, :] < lengths[:, None, None], (requests, query_rows, cache_span)
    )
    cache_part = block_partial(query, query_rope, cache_lat, cache_rope, cache_valid)
    token_of_row = lax.iota(jnp.int32, query_rows) // head_count
    fresh_valid = lax.iota(jnp.int32, new_steps)[None, :] <= token_of_row[:, None]
    fresh_valid = jnp.broadcast_to(fresh_valid[None, :, :], (requests, query_rows, new_steps))
    fresh_part = block_partial(query, query_rope, new_lat, new_rope, fresh_valid)
    merged = merged_2(cache_part, "blk", merge_pair)
    peak_val, weight_sum, summed = merge_pair(merged, fresh_part)
    lat_out = (summed / weight_sum[:, :, None]).astype(jnp.bfloat16)
    token_rows = requests * new_steps
    head_cols = w_uv.shape[1]
    head_pick = lax.axis_index("blk") * head_cols // V
    lat_heads = lat_out.reshape(requests, new_steps, head_count, latent_dim)
    lat_head = lax.dynamic_index_in_dim(lat_heads, head_pick, axis=2, keepdims=False).reshape(
        token_rows, latent_dim
    )
    heads_out = jnp.dot(lat_head, w_uv, preferred_element_type=jnp.float32).astype(jnp.bfloat16)
    proj_part = jnp.dot(heads_out, w_out, preferred_element_type=jnp.float32)
    projected = lax.psum(proj_part, "blk")
    width = hidden_in.shape[2]
    mixed = hidden_in.reshape(token_rows, width).astype(jnp.float32) + projected
    meansq = jnp.mean(mixed * mixed, axis=1, keepdims=True)
    normed = (mixed * lax.rsqrt(meansq + NORM_EPS) * norm_gain[None, :]).astype(jnp.bfloat16)
    affinity = jax.nn.sigmoid(jnp.dot(normed, w_router, preferred_element_type=jnp.float32))
    expert_total = w_router.shape[1]
    top_count = routes.shape[2]
    flat_routes = routes.reshape(token_rows, top_count)
    route_hits = flat_routes[:, :, None] == lax.iota(jnp.int32, expert_total)[None, None, :]
    chosen = jnp.sum(jnp.where(route_hits, affinity[:, None, :], 0.0), axis=2)
    route_weight = ROUTE_SCALE * chosen / jnp.sum(chosen, axis=1, keepdims=True)
    local_count = w_gate.shape[0]
    local_ids = lax.axis_index("blk") * local_count + lax.iota(jnp.int32, local_count)
    pair_routes = flat_routes.reshape(token_rows * top_count)
    local_hits = (pair_routes[:, None] == local_ids[None, :]).astype(jnp.int32)
    ranks = jnp.cumsum(local_hits, axis=0) - 1
    slot_ids = lax.iota(jnp.int32, CAP)
    slot_match = local_hits.T[:, None, :] * (ranks.T[:, None, :] == slot_ids[None, :, None]).astype(
        jnp.int32
    )
    select = slot_match.reshape(local_count, CAP, token_rows, top_count).astype(jnp.float32)
    dispatch_map = jnp.sum(select, axis=3)
    combine_map = jnp.sum(select * route_weight[None, None, :, :], axis=3)
    dispatched = jnp.einsum(
        "esr,rd->esd", dispatch_map.astype(jnp.bfloat16), normed, preferred_element_type=jnp.float32
    ).astype(jnp.bfloat16)
    piece = lax.all_gather(dispatched, "exp", axis=1, tiled=True)
    gate = jnp.einsum("erd,edf->erf", piece, w_gate, preferred_element_type=jnp.float32)
    upper = jnp.einsum("erd,edf->erf", piece, w_up, preferred_element_type=jnp.float32)
    hidden_all = (jax.nn.silu(gate) * upper).astype(jnp.bfloat16)
    partial_out = jnp.einsum("erf,efd->erd", hidden_all, w_down, preferred_element_type=jnp.float32)
    expert_out = lax.psum_scatter(partial_out, "exp", scatter_dimension=1, tiled=True)
    moe_part = jnp.einsum("esr,esd->rd", combine_map, expert_out, precision=lax.Precision.HIGHEST)
    moe_all = lax.psum(moe_part, "blk")
    result = (mixed + moe_all).astype(jnp.bfloat16)
    return result.reshape(requests, new_steps, width)


def solution(mesh):
    in_specs = (
        P("exp", None, None),
        P("exp", None, None, None),
        P("exp", None, None, None),
        P("exp", None, None),
        P("exp", None, None),
        P("exp", "blk", None),
        P("exp", "blk", None),
        P("exp"),
        P(None, "blk"),
        P("blk", None),
        P(),
        P(),
        P("exp", None, None),
        P("blk", None, "exp"),
        P("blk", None, "exp"),
        P("blk", "exp", None),
    )
    out_specs = P("exp", None, None)
    return jax.shard_map(local, mesh=mesh, in_specs=in_specs, out_specs=out_specs, check_vma=False)
```

profile of v0, /device:TPU:24, one launch (start us, length us, event | category | flops | bytes accessed | tf_op | source)
XLA Modules:
  0.0 1199.8 jit_solution(7835807839142678732)
XLA Ops:
  7.8 1.4 fusion.56
  11.8 70.6 %all-gather.5 = f32[64,4,64]{2,1,0:T(4,128)S(1)} all-gather(f32[1,4,64]{2,1,0:T(4,128)S(1)} %bitcast.74), channel_id=3, replica_groups=mesh['blk'=64,'exp'=8] {'blk'}, dimensions={0}, use_global_device_ids=true | all-gather | bytes 66560 | tf_op jit(solution)/shard_map/all_gather | solution.py:15
  82.4 61.4 %all-gather.4 = f32[64,4,64]{2,1,0:T(4,128)S(1)} all-gather(f32[1,4,64]{2,1,0:T(4,128)S(1)} %bitcast.73), channel_id=2, replica_groups=mesh['blk'=64,'exp'=8] {'blk'}, dimensions={0}, use_global_device_ids=true | all-gather | bytes 66560 | tf_op jit(solution)/shard_map/all_gather | solution.py:15
  146.7 65.1 %all-gather.9.cloned.1.call-done = f32[256,64,512]{2,1,0:T(8,128)} async-done(((f32[4,64,512]{2,1,0:T(8,128)}), f32[256,64,512]{2,1,0:T(8,128)}) %all-gather.9.cloned.1.call-update) | async-done | bytes 33554448 | tf_op jit(solution)/shard_map/all_gather | solution.py:15
  212.9 79.7 %while.19 = (s32[]{:T(128)}, f32[4,64]{1,0:T(4,128)S(1)}, f32[4,64]{1,0:T(4,128)S(1)}, f32[4,64,512]{2,1,0:T(8,128)S(1)}, f32[64,4,64]{2,1,0:T(4,128)S(1)}, /*in...) while((s32[]{:T(128)}, f32[4,64]{1,0:T(4,128)S(1)}, ...), condition=%wide.region_3.4_spmd, body=%wide.region_2.3_spmd.sunk | while | flops 394757 | bytes 1583255 | solution.py:21
  212.9 1.2 fusion.79
  214.2 1.2 fusion.79
  215.5 1.2 fusion.79
  220.5 1.2 fusion.79
  221.8 1.2 fusion.79
  223.1 1.2 fusion.79
  224.3 1.2 fusion.79
  228.1 1.2 fusion.79
  229.4 1.2 fusion.79
  230.7 1.2 fusion.79
  231.9 1.2 fusion.79
  235.7 1.2 fusion.79
  237.0 1.2 fusion.79
  238.2 1.2 fusion.79
  239.5 1.2 fusion.79
  244.6 1.2 fusion.79
  245.8 1.2 fusion.79
  247.1 1.2 fusion.79
  248.4 1.2 fusion.79
  252.2 1.2 fusion.79
  253.4 1.2 fusion.79
  254.7 1.2 fusion.79
  256.0 1.2 fusion.79
  259.8 1.2 fusion.79
  261.0 1.2 fusion.79
  262.3 1.2 fusion.79
  263.5 1.2 fusion.79
  268.6 1.2 fusion.79
  269.9 1.2 fusion.79
  271.1 1.2 fusion.79
  272.4 1.2 fusion.79
  276.2 1.2 fusion.79
  277.5 1.2 fusion.79
  278.7 1.2 fusion.79
  280.0 1.2 fusion.79
  293.8 1.9 fusion.15
  298.7 375.5 %all-reduce.5.cloned.1.call-done = f32[16,2048]{1,0:T(8,128)} async-done(((f32[16,2048]{1,0:T(8,128)}), f32[16,2048]{1,0:T(8,128)}) %all-reduce.5.cloned.1.call-update) | async-done | bytes 131088 | tf_op jit(solution)/shard_map/psum | solution.py:95
  677.6 34.2 %all-gather.6 = bf16[8,3,2048]{2,1,0:T(4,128)(2,1)S(1)} all-gather(bf16[1,3,2048]{2,1,0:T(4,128)(2,1)S(1)} %fusion.3), channel_id=5, replica_groups=mesh['blk'=64,'exp'=8] {'exp'}, dimensions={0}, use_global_device_ids=true | all-gather | bytes 110592 | tf_op jit(solution)/shard_map/all_gather | solution.py:122
  711.9 1.4 fusion.19
  713.3 2.0 convolution_bitcast_fusion
  716.3 1.3 dynamic-slice
  718.2 93.9 %all-reduce.9.cloned.1.call-done = f32[1,24,2048]{2,0,1:T(1,128)} async-done(((f32[1,24,2048]{2,0,1:T(1,128)}), f32[1,24,2048]{2,0,1:T(1,128)}) %all-reduce.9.cloned.1.call-update) | async-done | bytes 196624
  813.9 377.7 %all-reduce.7.cloned.1.call-done = f32[16,2048]{1,0:T(8,128)} async-done(((f32[16,2048]{1,0:T(8,128)}), f32[16,2048]{1,0:T(8,128)}) %all-reduce.7.cloned.1.call-update) | async-done | bytes 131088 | tf_op jit(solution)/shard_map/psum | solution.py:129
  (141 shorter events, 55.3 us)
Async XLA Ops:
  6.5 1.2 copy-start
  6.5 205.3 %all-gather.9.cloned.1.call-start = ((), (), s32[]{:S(2)}) async-start(), calls=%async_computation.2 | async-start | bytes 34078720 | tf_op jit(solution)/shard_map/all_gather | solution.py:15
  11.5 662.7 %all-reduce.5.cloned.1.call-start = ((), (), s32[]{:S(2)}) async-start(), calls=%async_computation | async-start | bytes 262144 | tf_op jit(solution)/shard_map/psum | solution.py:95
  295.7 516.5 %all-reduce.9.cloned.1.call-start = ((), (), s32[]{:S(2)}) async-start(), calls=%async_computation.3 | async-start | bytes 393216
  716.3 475.4 %all-reduce.7.cloned.1.call-start = ((), (), s32[]{:S(2)}) async-start(), calls=%async_computation.1 | async-start | bytes 262144 | tf_op jit(solution)/shard_map/psum | solution.py:129
Sparse Core Ops, SparseCore 0:
  11.6 200.1 all-gather.8
  295.8 378.3 all-reduce.4
  716.4 95.6 all-reduce.8
  814.9 376.7 all-reduce.6
where the time goes:
time: 1200 us
  waiting for transfers between devices  912 us (76%)
  blocking collectives  166 us (14%)
  other arithmetic  82.9 us (7%)
  matrix products  15.3 us (1%)
  between operations  13.9 us (1%)
    psum x1, waiting for transfers between devices, local(): moe_all = lax.psum(moe_part, 'blk')  378 us
    psum x1, waiting for transfers between devices, local(): projected = lax.psum(proj_part, 'blk')  376 us
    all_gather x2, blocking collectives, merged_2(): everything = jax.tree.map(lambda part: lax.all_gather(part, axis), x)  132 us
    unnamed x5, waiting for transfers between devices  94 us
    add x63, other arithmetic, merge_pair(): factor_left[..., None] * sum_left + factor_right[..., None] * sum_right  76.3 us
    all_gather x1, waiting for transfers between devices, merged_2(): everything = jax.tree.map(lambda part: lax.all_gather(part, axis), x)  65.1 us
    all_gather x1, blocking collectives, local(): piece = lax.all_gather(dispatched, 'exp', axis=1, tiled=True)  34.2 us
  transfers between devices with their start and end apart: 4, of which 4 were waited for; matrix products, arithmetic and copies ran while one was open for 1% of the time, Pallas kernels for 0%

commit v1 on v0

--- a/solution.py
+++ b/solution.py
@@ -92,7 +92,7 @@
     )
     heads_out = jnp.dot(lat_head, w_uv, preferred_element_type=jnp.float32).astype(jnp.bfloat16)
     proj_part = jnp.dot(heads_out, w_out, preferred_element_type=jnp.float32)
-    projected = lax.psum(proj_part, "blk")
+    projected = jnp.sum(jax.lax.all_gather(proj_part, "blk"), 0)
     width = hidden_in.shape[2]
     mixed = hidden_in.reshape(token_rows, width).astype(jnp.float32) + projected
     meansq = jnp.mean(mixed * mixed, axis=1, keepdims=True)

time: 1200 us -> 958 us (0.80)
  waiting for transfers between devices: 912 us -> 662 us
    psum x1 -> x0, waiting for transfers between devices: 376 us -> none  [local(): projected = lax.psum(proj_part, 'blk')]
    all_gather x0 -> x1, waiting for transfers between devices: none -> 125 us  [local(): projected = jnp.sum(jax.lax.all_gather(proj_part, 'blk'), 0)]
where the time goes in v1:
time: 958 us; the launch traced here: 954 us
  waiting for transfers between devices  662 us (69%)
  blocking collectives  166 us (17%)
  other arithmetic  88.5 us (9%)
  matrix products  14.5 us (2%)
  between operations  13.9 us (1%)
    psum x1, waiting for transfers between devices, local(): moe_all = lax.psum(moe_part, 'blk')  378 us
    all_gather x2, blocking collectives, merged_2(): everything = jax.tree.map(lambda part: lax.all_gather(part, axis), x)  132 us
    all_gather x1, waiting for transfers between devices, local(): projected = jnp.sum(jax.lax.all_gather(proj_part, 'blk'), 0)  125 us
    unnamed x5, waiting for transfers between devices  93.1 us
    add x63, other arithmetic, merge_pair(): factor_left[..., None] * sum_left + factor_right[..., None] * sum_right  77.2 us
    all_gather x1, waiting for transfers between devices, merged_2(): everything = jax.tree.map(lambda part: lax.all_gather(part, axis), x)  65.8 us
    all_gather x1, blocking collectives, local(): piece = lax.all_gather(dispatched, 'exp', axis=1, tiled=True)  34.2 us
  transfers between devices with their start and end apart: 4, of which 4 were waited for; matrix products, arithmetic and copies ran while one was open for 1% of the time, Pallas kernels for 0%

profile of v1, /device:TPU:24, one launch (start us, length us, event | category | flops | bytes accessed | tf_op | source)
XLA Modules:
  0.0 954.0 jit_solution(2277064533416841878)
XLA Ops:
  7.8 1.4 fusion.58
  11.8 70.6 %all-gather.6 = f32[64,4,64]{2,1,0:T(4,128)S(1)} all-gather(f32[1,4,64]{2,1,0:T(4,128)S(1)} %bitcast.77), channel_id=3, replica_groups=mesh['blk'=64,'exp'=8] {'blk'}, dimensions={0}, use_global_device_ids=true | all-gather | bytes 66560 | tf_op jit(solution)/shard_map/all_gather | solution.py:15
  82.4 61.4 %all-gather.5 = f32[64,4,64]{2,1,0:T(4,128)S(1)} all-gather(f32[1,4,64]{2,1,0:T(4,128)S(1)} %bitcast.76), channel_id=2, replica_groups=mesh['blk'=64,'exp'=8] {'blk'}, dimensions={0}, use_global_device_ids=true | all-gather | bytes 66560 | tf_op jit(solution)/shard_map/all_gather | solution.py:15
  146.0 65.8 %all-gather.11.cloned.1.call-done = f32[256,64,512]{2,1,0:T(8,128)} async-done(((f32[4,64,512]{2,1,0:T(8,128)}), f32[256,64,512]{2,1,0:T(8,128)}) %all-gather.11.cloned.1.call-update) | async-done | bytes 33554448 | tf_op jit(solution)/shard_map/all_gather | solution.py:15
  212.9 80.6 %while.19 = (s32[]{:T(128)}, f32[4,64]{1,0:T(4,128)S(1)}, f32[4,64]{1,0:T(4,128)S(1)}, f32[4,64,512]{2,1,0:T(8,128)S(1)}, f32[64,4,64]{2,1,0:T(4,128)S(1)}, /*in...) while((s32[]{:T(128)}, f32[4,64]{1,0:T(4,128)S(1)}, ...), condition=%wide.region_3.4_spmd, body=%wide.region_2.3_spmd.sunk | while | flops 394757 | bytes 1583255 | solution.py:21
  212.9 1.2 fusion.82
  214.2 1.2 fusion.82
  215.5 1.2 fusion.82
  216.8 1.2 fusion.82
  219.3 1.2 fusion.82
  220.6 1.2 fusion.82
  223.2 1.2 fusion.82
  224.4 1.2 fusion.82
  225.7 1.2 fusion.82
  227.0 1.2 fusion.82
  228.3 1.2 fusion.82
  229.6 1.2 fusion.82
  230.8 1.2 fusion.82
  233.4 1.2 fusion.82
  234.7 1.2 fusion.82
  236.0 1.2 fusion.82
  237.2 1.2 fusion.82
  238.5 1.2 fusion.82
  239.8 1.2 fusion.82
  241.1 1.2 fusion.82
  243.6 1.2 fusion.82
  244.9 1.2 fusion.82
  247.5 1.2 fusion.82
  248.7 1.2 fusion.82
  250.0 1.2 fusion.82
  251.3 1.2 fusion.82
  252.6 1.2 fusion.82
  253.9 1.2 fusion.82
  255.1 1.2 fusion.82
  257.7 1.2 fusion.82
  259.0 1.2 fusion.82
  260.3 1.2 fusion.82
  261.5 1.2 fusion.82
  262.8 1.2 fusion.82
  294.7 1.9 fusion.15
  300.3 124.9 %all-gather.13.cloned.1.call-done = f32[1024,2048]{1,0:T(8,128)} async-done(((f32[16,2048]{1,0:T(8,128)}), f32[1024,2048]{1,0:T(8,128)}) %all-gather.13.cloned.1.call-update) | async-done | bytes 8388624 | tf_op jit(solution)/shard_map/all_gather | solution.py:95
  425.1 3.8 reduce_sum.76
  432.7 34.2 %all-gather.7 = bf16[8,3,2048]{2,1,0:T(4,128)(2,1)S(1)} all-gather(bf16[1,3,2048]{2,1,0:T(4,128)(2,1)S(1)} %fusion.3), channel_id=6, replica_groups=mesh['blk'=64,'exp'=8] {'exp'}, dimensions={0}, use_global_device_ids=true | all-gather | bytes 110592 | tf_op jit(solution)/shard_map/all_gather | solution.py:122
  466.9 1.4 fusion.19
  468.3 2.0 convolution_bitcast_fusion
  471.3 1.3 dynamic-slice
  473.3 93.1 %all-reduce.6.cloned.1.call-done = f32[1,24,2048]{2,0,1:T(1,128)} async-done(((f32[1,24,2048]{2,0,1:T(1,128)}), f32[1,24,2048]{2,0,1:T(1,128)}) %all-reduce.6.cloned.1.call-update) | async-done | bytes 196624
  568.1 377.7 %all-reduce.4.cloned.1.call-done = f32[16,2048]{1,0:T(8,128)} async-done(((f32[16,2048]{1,0:T(8,128)}), f32[16,2048]{1,0:T(8,128)}) %all-reduce.4.cloned.1.call-update) | async-done | bytes 131088 | tf_op jit(solution)/shard_map/psum | solution.py:129
  (147 shorter events, 57.2 us)
Async XLA Ops:
  6.5 1.2 copy-start
  6.5 205.3 %all-gather.11.cloned.1.call-start = ((), (), s32[]{:S(2)}) async-start(), calls=%async_computation.1 | async-start | bytes 34078720 | tf_op jit(solution)/shard_map/all_gather | solution.py:15
  11.5 413.6 %all-gather.13.cloned.1.call-start = ((), (), s32[]{:S(2)}) async-start(), calls=%async_computation.2 | async-start | bytes 8519680 | tf_op jit(solution)/shard_map/all_gather | solution.py:95
  296.5 269.8 %all-reduce.6.cloned.1.call-start = ((), (), s32[]{:S(2)}) async-start(), calls=%async_computation.3 | async-start | bytes 393216
  471.3 474.6 %all-reduce.4.cloned.1.call-start = ((), (), s32[]{:S(2)}) async-start(), calls=%async_computation | async-start | bytes 262144 | tf_op jit(solution)/shard_map/psum | solution.py:129
Sparse Core Ops, SparseCore 0:
  11.6 200.1 all-gather.10
  296.7 128.4 all-gather.12
  471.4 94.8 all-reduce.5
  569.1 376.7 all-reduce.3

commit v2 on v0

--- a/solution.py
+++ b/solution.py
@@ -1,3 +1,4 @@
+import functools
 import jax
 import jax.numpy as jnp
 from jax import lax
@@ -9,6 +10,15 @@
 NEG_FILL = -1e30
 ROUTE_SCALE = 2.446
 NORM_EPS = 1e-06
+
+
+def measure_lots_all(content, comm_axis):
+    tmp = lax.axis_size(comm_axis)
+    seen_now = jnp.stack(tmp * [content])
+    return jnp.concatenate(lax.all_to_all(seen_now, comm_axis, 0, 0), axis=1)
+
+
+_play_windows = functools.partial(measure_lots_all, comm_axis="exp")
 
 
 def merged_2(x, axis, combine):
@@ -119,7 +129,7 @@
     dispatched = jnp.einsum(
         "esr,rd->esd", dispatch_map.astype(jnp.bfloat16), normed, preferred_element_type=jnp.float32
     ).astype(jnp.bfloat16)
-    piece = lax.all_gather(dispatched, "exp", axis=1, tiled=True)
+    piece = _play_windows(dispatched)
     gate = jnp.einsum("erd,edf->erf", piece, w_gate, preferred_element_type=jnp.float32)
     upper = jnp.einsum("erd,edf->erf", piece, w_up, preferred_element_type=jnp.float32)
     hidden_all = (jax.nn.silu(gate) * upper).astype(jnp.bfloat16)

time: 1200 us -> 1180 us (0.983)
  blocking collectives: 166 us -> 144 us
    all_gather x1 -> x0, blocking collectives: 34.2 us -> none  [local(): piece = lax.all_gather(dispatched, 'exp', axis=1, tiled=True)]
    all_to_all x0 -> x1, blocking collectives: none -> 12.1 us  [measure_lots_all(): return jnp.concatenate(lax.all_to_all(seen_now, comm_axis, 0, 0), axis=1)]
where the time goes in v2:
time: 1180 us
  waiting for transfers between devices  911 us (77%)
  blocking collectives  144 us (12%)
  other arithmetic  82.9 us (7%)
  matrix products  15.3 us (1%)
  between operations  13.9 us (1%)
    psum x1, waiting for transfers between devices, local(): moe_all = lax.psum(moe_part, 'blk')  378 us
    psum x1, waiting for transfers between devices, local(): projected = lax.psum(proj_part, 'blk')  376 us
    all_gather x2, blocking collectives, merged_2(): everything = jax.tree.map(lambda part: lax.all_gather(part, axis), x)  132 us
    unnamed x5, waiting for transfers between devices  92.8 us
    add x63, other arithmetic, merge_pair(): factor_left[..., None] * sum_left + factor_right[..., None] * sum_right  76.3 us
    all_gather x1, waiting for transfers between devices, merged_2(): everything = jax.tree.map(lambda part: lax.all_gather(part, axis), x)  65.1 us
  transfers between devices with their start and end apart: 4, of which 4 were waited for; matrix products, arithmetic and copies ran while one was open for 1% of the time, Pallas kernels for 0%

profile of v2, /device:TPU:24, one launch (start us, length us, event | category | flops | bytes accessed | tf_op | source)
XLA Modules:
  0.0 1176.6 jit_solution(10919101895567348391)
XLA Ops:
  7.8 1.4 fusion.55
  11.8 70.6 %all-gather.4 = f32[64,4,64]{2,1,0:T(4,128)S(1)} all-gather(f32[1,4,64]{2,1,0:T(4,128)S(1)} %bitcast.72), channel_id=3, replica_groups=mesh['blk'=64,'exp'=8] {'blk'}, dimensions={0}, use_global_device_ids=true | all-gather | bytes 66560 | tf_op jit(solution)/shard_map/all_gather | solution.py:25
  82.4 61.4 %all-gather.3 = f32[64,4,64]{2,1,0:T(4,128)S(1)} all-gather(f32[1,4,64]{2,1,0:T(4,128)S(1)} %bitcast.71), channel_id=2, replica_groups=mesh['blk'=64,'exp'=8] {'blk'}, dimensions={0}, use_global_device_ids=true | all-gather | bytes 66560 | tf_op jit(solution)/shard_map/all_gather | solution.py:25
  146.7 65.1 %all-gather.7.cloned.1.call-done = f32[256,64,512]{2,1,0:T(8,128)} async-done(((f32[4,64,512]{2,1,0:T(8,128)}), f32[256,64,512]{2,1,0:T(8,128)}) %all-gather.7.cloned.1.call-update) | async-done | bytes 33554448 | tf_op jit(solution)/shard_map/all_gather | solution.py:25
  212.9 79.7 %while.19 = (s32[]{:T(128)}, f32[4,64]{1,0:T(4,128)S(1)}, f32[4,64]{1,0:T(4,128)S(1)}, f32[4,64,512]{2,1,0:T(8,128)S(1)}, f32[64,4,64]{2,1,0:T(4,128)S(1)}, /*in...) while((s32[]{:T(128)}, f32[4,64]{1,0:T(4,128)S(1)}, ...), condition=%wide.region_3.4_spmd, body=%wide.region_2.3_spmd.sunk | while | flops 394757 | bytes 1583255 | solution.py:31
  212.9 1.2 fusion.78
  214.2 1.2 fusion.78
  215.5 1.2 fusion.78
  220.5 1.2 fusion.78
  221.8 1.2 fusion.78
  223.1 1.2 fusion.78
  224.3 1.2 fusion.78
  228.1 1.2 fusion.78
  229.4 1.2 fusion.78
  230.7 1.2 fusion.78
  231.9 1.2 fusion.78
  235.7 1.2 fusion.78
  237.0 1.2 fusion.78
  238.2 1.2 fusion.78
  239.5 1.2 fusion.78
  244.6 1.2 fusion.78
  245.8 1.2 fusion.78
  247.1 1.2 fusion.78
  248.4 1.2 fusion.78
  252.2 1.2 fusion.78
  253.4 1.2 fusion.78
  254.7 1.2 fusion.78
  256.0 1.2 fusion.78
  259.8 1.2 fusion.78
  261.0 1.2 fusion.78
  262.3 1.2 fusion.78
  263.5 1.2 fusion.78
  268.6 1.2 fusion.78
  269.9 1.2 fusion.78
  271.1 1.2 fusion.78
  272.4 1.2 fusion.78
  276.2 1.2 fusion.78
  277.5 1.2 fusion.78
  278.7 1.2 fusion.78
  280.0 1.2 fusion.78
  293.8 1.9 fusion.14
  298.7 375.5 %all-reduce.5.cloned.1.call-done = f32[16,2048]{1,0:T(8,128)} async-done(((f32[16,2048]{1,0:T(8,128)}), f32[16,2048]{1,0:T(8,128)}) %all-reduce.5.cloned.1.call-update) | async-done | bytes 131088 | tf_op jit(solution)/shard_map/psum | solution.py:105
  677.7 12.1 %all_to_all.5 = bf16[8,1,3,2048]{3,2,1,0:T(4,128)(2,1)S(1)} all-to-all(bf16[8,1,3,2048]{3,2,1,0:T(4,128)(2,1)S(1)} %stack.2), channel_id=1, replica_groups=mesh['blk'=64,'exp'=8] {'exp'}, dimensions={0} | all-to-all | bytes 196608 | tf_op jit(solution)/shard_map/all_to_all | solution.py:18
  689.9 1.4 fusion.18
  691.3 2.0 convolution_bitcast_fusion
  694.3 1.3 dynamic-slice
  696.2 92.7 %all-reduce.9.cloned.1.call-done = f32[1,24,2048]{2,0,1:T(1,128)} async-done(((f32[1,24,2048]{2,0,1:T(1,128)}), f32[1,24,2048]{2,0,1:T(1,128)}) %all-reduce.9.cloned.1.call-update) | async-done | bytes 196624
  790.7 377.7 %all-reduce.7.cloned.1.call-done = f32[16,2048]{1,0:T(8,128)} async-done(((f32[16,2048]{1,0:T(8,128)}), f32[16,2048]{1,0:T(8,128)}) %all-reduce.7.cloned.1.call-update) | async-done | bytes 131088 | tf_op jit(solution)/shard_map/psum | solution.py:139
  (142 shorter events, 55.3 us)
Async XLA Ops:
  6.5 1.2 copy-start
  6.5 205.3 %all-gather.7.cloned.1.call-start = ((), (), s32[]{:S(2)}) async-start(), calls=%async_computation.3 | async-start | bytes 34078720 | tf_op jit(solution)/shard_map/all_gather | solution.py:25
  11.5 662.7 %all-reduce.5.cloned.1.call-start = ((), (), s32[]{:S(2)}) async-start(), calls=%async_computation.1 | async-start | bytes 262144 | tf_op jit(solution)/shard_map/psum | solution.py:105
  295.7 493.3 %all-reduce.9.cloned.1.call-start = ((), (), s32[]{:S(2)}) async-start(), calls=%async_computation.4 | async-start | bytes 393216
  694.3 474.2 %all-reduce.7.cloned.1.call-start = ((), (), s32[]{:S(2)}) async-start(), calls=%async_computation.2 | async-start | bytes 262144 | tf_op jit(solution)/shard_map/psum | solution.py:139
Sparse Core Ops, SparseCore 0:
  11.6 200.1 all-gather.6
  295.8 378.3 all-reduce.4
  694.4 94.5 all-reduce.8
  791.7 376.7 all-reduce.6
